TPU v7x, 256 devices: a whole 4x4x8 slice. The times are simulated.
256 devices in a mesh: segment: 4 (over x), dp: 64 (over y, z, core).
Axes of the slice: x: 4, y: 4, z: 8, core: 2. Of those that a mesh axis runs over, the one named last changes fastest.
Arguments:
- tokens: bfloat16 [32768, 8192], P('dp', 'segment'), may hold values from -16 to 16
- block_values: bfloat16 [8192, 768], P('segment'), may hold values from -0.09375 to 0.09375
- column_blocks: int32 [128, 12], P('segment'), may hold values from 0 to 15, as said below
- counts: int32 [128], P('segment'), may hold values from 4 to 12, as said below
- cotangent: bfloat16 [32768, 1024], P(('dp', 'segment')), may hold values from -6 to 6
Outputs:
- activation: bfloat16 [32768, 1024], P(('dp', 'segment'))
- input_grad: bfloat16 [32768, 8192], P('dp', 'segment')
- weight_grad: float32 [8192, 768], P(('segment', 'dp'))
Inputs may be any that keep to these rules, and one draw needn't show every extreme that they name: `column_blocks`: the first counts[r] entries of row r are distinct column blocks; entries at later slots are column blocks too and are ignored. `counts`: some row block uses all 12 slots.
All inputs are finite; a program needn't handle non-finite values.
Results may differ from a plain program's by a relative error of at most 0.001.
Values may be sent and summed in bfloat16 or wider, within the bound.
No kernel may reach another device: no remote copies, remote signals or barrier semaphores. Data moves between devices by JAX's collectives and lax.ppermute only.
A program may use at most 128 MiB of HBM per device.

v0:
```python
import jax
import jax.numpy as jnp
from jax import lax
from jax.sharding import PartitionSpec as P


def block_onehot(column_blocks, counts, col_blocks):
    slots = column_blocks.shape[1]
    named = column_blocks[:, :, None] == jnp.arange(col_blocks, dtype=jnp.int32)[None, None, :]
    alive = jnp.arange(slots, dtype=jnp.int32)[None, :, None] < counts[:, None, None]
    return named & alive


def select_slots(dense_rows, first_row, column_blocks, counts, block, col_blocks):
    row_count = dense_rows.shape[0]
    slots = column_blocks.shape[1]
    row_block = (first_row + jnp.arange(row_count, dtype=jnp.int32)) // block
    block_ids = jnp.take(column_blocks, row_block, axis=0)
    live_count = jnp.take(counts, row_block, axis=0)
    onehot = block_onehot(block_ids, live_count, col_blocks).astype(jnp.float32)
    picked = jnp.einsum(
        "rkc,rcj->rkj",
        onehot,
        dense_rows.reshape(row_count, col_blocks, block),
        precision=lax.Precision.HIGHEST,
    )
    return picked.reshape(row_count, slots * block)


def per_device(tokens, block_values, column_blocks, counts, cotangent):
    local_rows, features = tokens.shape
    width = cotangent.shape[1]
    row_blocks, slots = column_blocks.shape
    block = features // row_blocks
    col_blocks = width // block
    sections = lax.axis_size("segment")
    replicas = lax.axis_size("dp")
    onehot = block_onehot(column_blocks, counts, col_blocks).astype(jnp.bfloat16)
    blocks_view = block_values.reshape(row_blocks, block, slots, block)
    weight = (
        jnp.einsum("bkc,bikj->bicj", onehot, blocks_view, preferred_element_type=jnp.float32)
        .astype(jnp.bfloat16)
        .reshape(features, width)
    )
    share_rows = local_rows // sections
    own_start = lax.axis_index("segment") * share_rows
    partial_value = jnp.dot(tokens, weight, preferred_element_type=jnp.float32)
    preact_all = lax.psum(partial_value, "segment")
    cotangent_all = lax.all_gather(cotangent, "segment", axis=0, tiled=True)
    activation = lax.dynamic_slice_in_dim(preact_all, own_start, share_rows, 0).astype(jnp.bfloat16)
    owned_rows = features // replicas
    product = lax.dot_general(
        tokens, cotangent_all, (((0,), (0,)), ((), ())), preferred_element_type=jnp.float32
    )
    summed = lax.psum_scatter(product / replicas, "dp", scatter_dimension=0, tiled=True)
    weight_grad = select_slots(
        summed, lax.axis_index("dp") * owned_rows, column_blocks, counts, block, col_blocks
    )
    input_grad = lax.dot_general(
        cotangent_all, weight, (((1,), (1,)), ((), ())), preferred_element_type=jnp.float32
    ).astype(jnp.bfloat16)
    return (activation, input_grad, weight_grad)


def solution(mesh):
    in_specs = (
        P("dp", "segment"),
        P("segment", None),
        P("segment", None),
        P("segment"),
        P(("dp", "segment"), None),
    )
    out_specs = (P(("dp", "segment"), None), P("dp", "segment"), P(("segment", "dp"), None))
    return jax.shard_map(
        per_device, mesh=mesh, in_specs=in_specs, out_specs=out_specs, check_vma=False
    )
```

profile of v0, /device:TPU:2, one launch (start us, length us, event | category | flops | bytes accessed | tf_op | source)
XLA Modules:
  0.0 208.3 jit_solution(9606807791745923992)
XLA Ops:
  7.2 0.0 copy-start
  7.2 0.0 all-gather.2.cloned.1.call-start
  7.2 0.7 all-gather.2.cloned.1.call-update
  7.9 0.0 reduce-scatter.2.cloned.1.call-start
  8.0 30.3 %all-gather.2.cloned.1.call-done = bf16[512,1024]{1,0:T(8,128)(2,1)} async-done(((bf16[128,1024]{1,0:T(8,128)(2,1)}), bf16[512,1024]{1,0:T(8,128)(2,1)}) %all-gather.2.cloned.1.call-update) | async-done | bytes 1048592 | tf_op jit(solution)/shard_map/all_gather | solution.py:49
  38.3 0.0 copy-done
  38.3 6.8 %convolution_multiply_fusion = f32[2048,1024]{1,0:T(8,128)} fusion(bf16[512,2048]{1,0:T(8,128)(2,1)S(1)} %copy-done, bf16[512,1024]{1,0:T(8,128)(2,1)} %all-gather.2.cloned.1.call-done), kind=kOutput, calls=%fused_computation.3 | convolution fusion | flops 2149580800 | bytes 11534336 | tf_op jit(solution)/shard_map/dot_general | solution.py:52
  45.1 0.0 reduce-scatter.2.cloned.1.call-update
  45.1 0.0 copy-start.2
  45.1 0.0 copy-start.1
  45.1 10.6 %reshape.199 = bf16[32,64,12,64]{3,2,1,0:T(8,128)(2,1)} reshape(bf16[2048,768]{1,0:T(8,128)(2,1)} %param.6) | data formatting | bytes 6291456 | tf_op jit(solution)/shard_map/reshape | solution.py:39
  55.7 0.0 copy-done.2
  55.7 0.1 copy.12
  55.9 0.6 gather_fusion
  56.4 0.0 copy-done.1
  56.4 0.7 gather_fusion.1
  57.1 0.1 iota_compare_fusion.3
  57.2 9.1 %convert_bitcast_fusion = bf16[32,64,16,64]{3,2,1,0:T(8,128)(2,1)} fusion(bf16[32,64,12,64]{3,2,1,0:T(8,128)(2,1)} %reshape.199, s32[32,12]{1,0:T(8,128)S(1)} %copy.12, pred[32,12]{1,0:T(8,128)(4,1)S(1)} %iota_compare_fusion.3), kind=kOutput, calls=%fused_computation.2 | convolution fusion | flops 52441088 | bytes 7341952 | tf_op jit(solution)/shard_map/bkc,bikj->bicj/dot_general | solution.py:41
  66.3 12.0 %reshape.179 = bf16[2048,1024]{1,0:T(8,128)(2,1)} reshape(bf16[32,64,16,64]{3,2,1,0:T(8,128)(2,1)} %convert_bitcast_fusion) | data formatting | bytes 8388608 | tf_op jit(solution)/shard_map/reshape | solution.py:43
  78.3 6.0 %convolution_bitcast_fusion = f32[512,1024]{0,1:T(8,128)} fusion(bf16[2048,1024]{1,0:T(8,128)(2,1)} %reshape.179, bf16[512,2048]{1,0:T(8,128)(2,1)S(1)} %copy-done), kind=kOutput, calls=%fused_computation.6 | convolution fusion | flops 2147483648 | bytes 8388608 | tf_op jit(solution)/shard_map/dot_general | solution.py:47
  84.3 41.4 %all-reduce.1 = bf16[512,1024]{0,1:T(8,128)(2,1)S(1)} all-reduce(f32[512,1024]{0,1:T(8,128)} %convolution_bitcast_fusion), channel_id=1, replica_groups=mesh['segment'=4,'dp'=64] {'segment'}, use_global_device_ids=true, to_apply=%region_0.0 | all-reduce | flops 524288 | bytes 3145728 | tf_op jit(solution)/shard_map/psum | solution.py:48
  125.8 0.9 copy.16
  126.7 0.1 iota_compare_fusion.2
  126.8 0.1 broadcast_select_fusion
  126.9 6.2 %fusion = bf16[512,2048]{0,1:T(8,128)(2,1)} fusion(bf16[2048,1024]{1,0:T(8,128)(2,1)} %reshape.179, bf16[512,1024]{1,0:T(8,128)(2,1)} %all-gather.2.cloned.1.call-done), kind=kOutput, calls=%fused_computation.5 | convolution fusion | flops 2148532224 | bytes 7340032 | tf_op jit(solution)/shard_map/dot_general | solution.py:59
  133.1 3.9 %copy.17 = bf16[512,2048]{1,0:T(8,128)(2,1)} copy(bf16[512,2048]{0,1:T(8,128)(2,1)} %fusion) | data formatting | bytes 4194304
  137.0 62.2 %reduce-scatter.2.cloned.1.call-done = f32[32,1024]{1,0:T(8,128)} async-done(((f32[2048,1024]{1,0:T(8,128)}), f32[32,1024]{1,0:T(8,128)}) %reduce-scatter.2.cloned.1.call-update) | async-done | bytes 131088 | tf_op jit(solution)/shard_map/reduce_scatter | solution.py:55
  199.3 1.0 reshape.180
  200.3 0.4 fusion.5
  200.7 0.7 reshape.181
  (5 shorter events, 0.1 us)
Async XLA Ops:
  7.2 31.1 %copy-start = (bf16[512,2048]{1,0:T(8,128)(2,1)S(1)}, bf16[512,2048]{1,0:T(8,128)(2,1)}, u32[]{:S(2)}) copy-start(bf16[512,2048]{1,0:T(8,128)(2,1)} %param.5) | copy-start | bytes 6291460
  7.2 31.1 %all-gather.2.cloned.1.call-start = ((), (), s32[]{:S(2)}) async-start(), calls=%async_computation.1 | async-start | bytes 1310720 | tf_op jit(solution)/shard_map/all_gather | solution.py:49
  7.9 191.3 %reduce-scatter.2.cloned.1.call-start = ((), (), s32[]{:S(2)}) async-start(), calls=%async_computation.2 | async-start | bytes 8519680 | tf_op jit(solution)/shard_map/reduce_scatter | solution.py:55
  45.1 10.6 %copy-start.2 = (s32[32,12]{0,1:T(8,128)S(1)}, s32[32,12]{0,1:T(8,128)}, u32[]{:S(2)}) copy-start(s32[32,12]{0,1:T(8,128)} %param.7) | copy-start | bytes 4612
  45.1 11.3 %copy-start.1 = (s32[32]{0:T(128)S(1)}, s32[32]{0:T(128)}, u32[]{:S(2)}) copy-start(s32[32]{0:T(128)} %param.8) | copy-start | bytes 388
Sparse Core Ops, SparseCore 0:
  9.8 28.4 all-gather.1
  45.2 153.9 reduce-scatter.1
where the time goes:
time: 209 us; the launch traced here: 208 us
  waiting for transfers between devices  93.2 us (45%)
  blocking collectives  41.4 us (20%)
  local copies, waits for them, and re-layouts  30.6 us (15%)
  matrix products  28.6 us (14%)
  between operations  14.1 us (7%)
    reduce_scatter x1, waiting for transfers between devices, per_device(): lax.psum_scatter(product / replicas, 'dp', scatter_dimension=0, tiled=True)  62.2 us
    psum x1, blocking collectives, per_device(): preact_all = lax.psum(partial_value, 'segment')  41.4 us
    all_gather x1, waiting for transfers between devices, per_device(): cotangent_all = lax.all_gather(cotangent, 'segment', axis=0, tiled=True)  30.3 us
    reshape x1, local copies, waits for them, and re-layouts, per_device(): weight = jnp.einsum('bkc,bikj->bicj', onehot, blocks_view, preferred_elem...  12 us
    reshape x1, local copies, waits for them, and re-layouts, per_device(): blocks_view = block_values.reshape(row_blocks, block, slots, block)  10.6 us
    dot_general x1, matrix products, per_device(): jnp.einsum('bkc,bikj->bicj', onehot, blocks_view, preferred_element_type=...  9.11 us
    dot_general x1, matrix products, per_device(): lax.dot_general(tokens, cotangent_all, (((0,), (0,)), ((), ())), preferre...  6.82 us
    dot_general x1, matrix products, per_device(): lax.dot_general(cotangent_all, weight, (((1,), (1,)), ((), ())), preferre...  6.23 us
  transfers between devices with their start and end apart: 2, of which 2 were waited for; matrix products, arithmetic and copies ran while one was open for 24% of the time, Pallas kernels for 0%

commit v1 on v0

--- a/solution.py
+++ b/solution.py
@@ -46,7 +46,9 @@
     own_start = lax.axis_index("segment") * share_rows
     partial_value = jnp.dot(tokens, weight, preferred_element_type=jnp.float32)
     preact_all = lax.psum(partial_value, "segment")
-    cotangent_all = lax.all_gather(cotangent, "segment", axis=0, tiled=True)
+    cotangent_all = jnp.concatenate(
+        lax.all_to_all(jnp.stack([cotangent] * lax.axis_size("segment")), "segment", 0, 0), axis=0
+    )
     activation = lax.dynamic_slice_in_dim(preact_all, own_start, share_rows, 0).astype(jnp.bfloat16)
     owned_rows = features // replicas
     product = lax.dot_general(

time: 209 us -> 198 us (0.947)
  waiting for transfers between devices: 93.2 us -> 62.5 us
  blocking collectives: 41.4 us -> 59.9 us
  local copies, waits for them, and re-layouts: 30.6 us -> 32.8 us
    all_gather x1 -> x0, waiting for transfers between devices: 30.3 us -> none  [per_device(): cotangent_all = lax.all_gather(cotangent, 'segment', axis=0, tiled=True)]
    all_to_all x0 -> x1, blocking collectives: none -> 18.3 us  [per_device(): lax.all_to_all(jnp.stack([cotangent] * lax.axis_size('segment')), 'segmen...]
    unnamed x9 -> x11, local copies, waits for them, and re-layouts: 4.89 us -> 5.94 us
  transfers between devices with their start and end apart: 2 -> 1, of which waited for: 2 -> 1; matrix products, arithmetic and copies ran while one was open for 24% -> 26% of each run, Pallas kernels for 0% -> 0%
where the time goes in v1:
time: 198 us; the launch traced here: 197 us
  waiting for transfers between devices  62.5 us (32%)
  blocking collectives  59.9 us (30%)
  local copies, waits for them, and re-layouts  32.8 us (17%)
  matrix products  27.4 us (14%)
  between operations  14.1 us (7%)
    reduce_scatter x1, waiting for transfers between devices, per_device(): lax.psum_scatter(product / replicas, 'dp', scatter_dimension=0, tiled=True)  62.4 us
    psum x1, blocking collectives, per_device(): preact_all = lax.psum(partial_value, 'segment')  41.6 us
    all_to_all x1, blocking collectives, per_device(): lax.all_to_all(jnp.stack([cotangent] * lax.axis_size('segment')), 'segmen...  18.3 us
    reshape x1, local copies, waits for them, and re-layouts, per_device(): weight = jnp.einsum('bkc,bikj->bicj', onehot, blocks_view, preferred_elem...  12 us
    reshape x1, local copies, waits for them, and re-layouts, per_device(): blocks_view = block_values.reshape(row_blocks, block, slots, block)  10.6 us
    dot_general x1, matrix products, per_device(): jnp.einsum('bkc,bikj->bicj', onehot, blocks_view, preferred_element_type=...  9.14 us
    dot_general x1, matrix products, per_device(): lax.dot_general(cotangent_all, weight, (((1,), (1,)), ((), ())), preferre...  6.25 us
    dot_general x1, matrix products, per_device(): partial_value = jnp.dot(tokens, weight, preferred_element_type=jnp.float32)  6.01 us
  transfers between devices with their start and end apart: 1, of which 1 were waited for; matrix products, arithmetic and copies ran while one was open for 26% of the time, Pallas kernels for 0%

profile of v1, /device:TPU:2, one launch (start us, length us, event | category | flops | bytes accessed | tf_op | source)
XLA Modules:
  0.0 196.9 jit_solution(832957169809104598)
XLA Ops:
  7.2 0.0 copy-start
  7.2 0.0 reduce-scatter.2.cloned.1.call-start
  7.2 1.2 stack.2
  8.4 18.3 %all_to_all.5 = bf16[4,128,1024]{2,1,0:T(8,128)(2,1)S(1)} all-to-all(bf16[4,128,1024]{2,1,0:T(8,128)(2,1)S(1)} %stack.2), channel_id=1, replica_groups=mesh['segment'=4,'dp'=64] {'segment'}, dimensions={0} | all-to-all | bytes 2097152 | tf_op jit(solution)/shard_map/all_to_all | solution.py:50
  26.7 0.0 copy-start.2
  26.7 1.0 copy-done.2
  27.8 0.0 copy-done
  27.8 5.6 %convolution_multiply_fusion = f32[2048,1024]{1,0:T(8,128)} fusion(bf16[512,2048]{1,0:T(8,128)(2,1)S(1)} %copy-done, bf16[512,1024]{1,0:T(8,128)(2,1)S(1)} %bitcast.24), kind=kOutput, calls=%fused_computation.3 | convolution fusion | flops 2149580800 | bytes 11534336 | tf_op jit(solution)/shard_map/dot_general | solution.py:54
  33.4 0.0 reduce-scatter.2.cloned.1.call-update
  33.4 0.0 copy-start.3
  33.4 0.0 copy-start.1
  33.4 10.6 %reshape.205 = bf16[32,64,12,64]{3,2,1,0:T(8,128)(2,1)} reshape(bf16[2048,768]{1,0:T(8,128)(2,1)} %param.6) | data formatting | bytes 6291456 | tf_op jit(solution)/shard_map/reshape | solution.py:39
  44.0 0.0 copy-done.3
  44.0 0.1 copy.12
  44.1 0.6 gather_fusion
  44.7 0.0 copy-done.1
  44.7 0.7 gather_fusion.1
  45.4 0.1 iota_compare_fusion.3
  45.5 9.1 %convert_bitcast_fusion = bf16[32,64,16,64]{3,2,1,0:T(8,128)(2,1)} fusion(bf16[32,64,12,64]{3,2,1,0:T(8,128)(2,1)} %reshape.205, s32[32,12]{1,0:T(8,128)S(1)} %copy.12, pred[32,12]{1,0:T(8,128)(4,1)S(1)} %iota_compare_fusion.3), kind=kOutput, calls=%fused_computation.2 | convolution fusion | flops 52441088 | bytes 7341952 | tf_op jit(solution)/shard_map/bkc,bikj->bicj/dot_general | solution.py:41
  54.6 12.0 %reshape.184 = bf16[2048,1024]{1,0:T(8,128)(2,1)} reshape(bf16[32,64,16,64]{3,2,1,0:T(8,128)(2,1)} %convert_bitcast_fusion) | data formatting | bytes 8388608 | tf_op jit(solution)/shard_map/reshape | solution.py:43
  66.6 6.0 %convolution_bitcast_fusion = f32[512,1024]{0,1:T(8,128)} fusion(bf16[2048,1024]{1,0:T(8,128)(2,1)} %reshape.184, bf16[512,2048]{1,0:T(8,128)(2,1)S(1)} %copy-done), kind=kOutput, calls=%fused_computation.6 | convolution fusion | flops 2147483648 | bytes 8388608 | tf_op jit(solution)/shard_map/dot_general | solution.py:47
  72.6 41.6 %all-reduce.1 = bf16[512,1024]{0,1:T(8,128)(2,1)S(1)} all-reduce(f32[512,1024]{0,1:T(8,128)} %convolution_bitcast_fusion), channel_id=1, replica_groups=mesh['segment'=4,'dp'=64] {'segment'}, use_global_device_ids=true, to_apply=%region_0.0 | all-reduce | flops 524288 | bytes 3145728 | tf_op jit(solution)/shard_map/psum | solution.py:48
  114.3 0.9 copy.16
  115.1 0.1 iota_compare_fusion.2
  115.2 0.1 broadcast_select_fusion
  115.3 6.2 %fusion = bf16[512,2048]{0,1:T(8,128)(2,1)} fusion(bf16[2048,1024]{1,0:T(8,128)(2,1)} %reshape.184, bf16[512,1024]{1,0:T(8,128)(2,1)} %bitcast.25), kind=kOutput, calls=%fused_computation.5 | convolution fusion | flops 2148532224 | bytes 7340032 | tf_op jit(solution)/shard_map/dot_general | solution.py:61
  121.5 3.9 %copy.17 = bf16[512,2048]{1,0:T(8,128)(2,1)} copy(bf16[512,2048]{0,1:T(8,128)(2,1)} %fusion) | data formatting | bytes 4194304
  125.5 62.4 %reduce-scatter.2.cloned.1.call-done = f32[32,1024]{1,0:T(8,128)} async-done(((f32[2048,1024]{1,0:T(8,128)}), f32[32,1024]{1,0:T(8,128)}) %reduce-scatter.2.cloned.1.call-update) | async-done | bytes 131088 | tf_op jit(solution)/shard_map/reduce_scatter | solution.py:57
  187.9 1.0 reshape.186
  188.9 0.4 fusion.5
  189.3 0.7 reshape.187
  (5 shorter events, 0.1 us)
Async XLA Ops:
  7.2 20.6 %copy-start = (bf16[512,2048]{1,0:T(8,128)(2,1)S(1)}, bf16[512,2048]{1,0:T(8,128)(2,1)}, u32[]{:S(2)}) copy-start(bf16[512,2048]{1,0:T(8,128)(2,1)} %param.5) | copy-start | bytes 6291460
  7.2 180.7 %reduce-scatter.2.cloned.1.call-start = ((), (), s32[]{:S(2)}) async-start(), calls=%async_computation.2 | async-start | bytes 8519680 | tf_op jit(solution)/shard_map/reduce_scatter | solution.py:57
  26.7 1.0 copy-start.2
  33.4 10.6 %copy-start.3 = (s32[32,12]{0,1:T(8,128)S(1)}, s32[32,12]{0,1:T(8,128)}, u32[]{:S(2)}) copy-start(s32[32,12]{0,1:T(8,128)} %param.7) | copy-start | bytes 4612
  33.4 11.3 %copy-start.1 = (s32[32]{0:T(128)S(1)}, s32[32]{0:T(128)}, u32[]{:S(2)}) copy-start(s32[32]{0:T(128)} %param.8) | copy-start | bytes 388
Sparse Core Ops, SparseCore 0:
  33.5 154.3 reduce-scatter.1

commit v2 on v0

--- a/solution.py
+++ b/solution.py
@@ -45,7 +45,7 @@
     share_rows = local_rows // sections
     own_start = lax.axis_index("segment") * share_rows
     partial_value = jnp.dot(tokens, weight, preferred_element_type=jnp.float32)
-    preact_all = lax.psum(partial_value, "segment")
+    preact_all = jnp.sum(lax.all_gather(partial_value, "segment"), axis=0)
     cotangent_all = lax.all_gather(cotangent, "segment", axis=0, tiled=True)
     activation = lax.dynamic_slice_in_dim(preact_all, own_start, share_rows, 0).astype(jnp.bfloat16)
     owned_rows = features // replicas

time: 209 us -> 302 us (1.44)
  waiting for transfers between devices: 93.2 us -> 208 us
  blocking collectives: 41.4 us -> 0 us
  local copies, waits for them, and re-layouts: 30.6 us -> 42.2 us
  other arithmetic: 0.27 us -> 8.74 us
    reduce_scatter x1, waiting for transfers between devices: 62.2 us -> 137 us  [per_device(): lax.psum_scatter(product / replicas, 'dp', scatter_dimension=0, tiled=True)]
    all_gather x0 -> x1, waiting for transfers between devices: none -> 70.1 us  [per_device(): preact_all = jnp.sum(lax.all_gather(partial_value, 'segment'), axis=0)]
    psum x1 -> x0, blocking collectives: 41.4 us -> none  [per_device(): preact_all = lax.psum(partial_value, 'segment')]
    all_gather x1, waiting for transfers between devices: 30.3 us -> 0.02 us  [per_device(): cotangent_all = lax.all_gather(cotangent, 'segment', axis=0, tiled=True)]
    all_gather x0 -> x1, local copies, waits for them, and re-layouts: none -> 10.8 us  [per_device(): preact_all = jnp.sum(lax.all_gather(partial_value, 'segment'), axis=0)]
    reduce_sum x0 -> x1, other arithmetic: none -> 8.47 us  [per_device(): preact_all = jnp.sum(lax.all_gather(partial_value, 'segment'), axis=0)]
  transfers between devices with their start and end apart: 2 -> 3, of which waited for: 2 -> 2; matrix products, arithmetic and copies ran while one was open for 24% -> 25% of each run, Pallas kernels for 0% -> 0%
where the time goes in v2:
time: 302 us; the launch traced here: 301 us
  waiting for transfers between devices  208 us (69%)
  local copies, waits for them, and re-layouts  42.2 us (14%)
  matrix products  28 us (9%)
  between operations  13.8 us (5%)
  other arithmetic  8.74 us (3%)
    reduce_scatter x1, waiting for transfers between devices, per_device(): lax.psum_scatter(product / replicas, 'dp', scatter_dimension=0, tiled=True)  137 us
    all_gather x1, waiting for transfers between devices, per_device(): preact_all = jnp.sum(lax.all_gather(partial_value, 'segment'), axis=0)  70.1 us
    reshape x1, local copies, waits for them, and re-layouts, per_device(): weight = jnp.einsum('bkc,bikj->bicj', onehot, blocks_view, preferred_elem...  11.9 us
    all_gather x1, local copies, waits for them, and re-layouts, per_device(): preact_all = jnp.sum(lax.all_gather(partial_value, 'segment'), axis=0)  10.8 us
    reshape x1, local copies, waits for them, and re-layouts, per_device(): blocks_view = block_values.reshape(row_blocks, block, slots, block)  10.6 us
    dot_general x1, matrix products, per_device(): jnp.einsum('bkc,bikj->bicj', onehot, blocks_view, preferred_element_type=...  8.92 us
    reduce_sum x1, other arithmetic, per_device(): preact_all = jnp.sum(lax.all_gather(partial_value, 'segment'), axis=0)  8.47 us
    dot_general x1, matrix products, per_device(): lax.dot_general(tokens, cotangent_all, (((0,), (0,)), ((), ())), preferre...  6.83 us
  transfers between devices with their start and end apart: 3, of which 2 were waited for; matrix products, arithmetic and copies ran while one was open for 25% of the time, Pallas kernels for 0%

profile of v2, /device:TPU:2, one launch (start us, length us, event | category | flops | bytes accessed | tf_op | source)
XLA Modules:
  0.0 301.2 jit_solution(3028232382280027868)
XLA Ops:
  7.2 0.0 copy-start
  7.2 0.0 all-gather.4.cloned.1.call-start
  7.2 0.7 all-gather.4.cloned.1.call-update
  7.9 0.0 all-gather.6.cloned.1.call-start
  8.0 0.8 copy.16
  8.7 10.6 %reshape.200 = bf16[32,64,12,64]{3,2,1,0:T(8,128)(2,1)} reshape(bf16[2048,768]{1,0:T(8,128)(2,1)} %param.6) | data formatting | bytes 6291456 | tf_op jit(solution)/shard_map/reshape | solution.py:39
  19.4 0.0 copy-done.1
  19.4 0.1 iota_compare_fusion.3
  19.4 8.9 %convert_bitcast_fusion = bf16[32,64,16,64]{3,2,1,0:T(8,128)(2,1)} fusion(bf16[32,64,12,64]{3,2,1,0:T(8,128)(2,1)} %reshape.200, s32[32,12]{1,0:T(8,128)S(1)} %copy.16, pred[32,12]{1,0:T(8,128)(4,1)S(1)} %iota_compare_fusion.3), kind=kOutput, calls=%fused_computation.2 | convolution fusion | flops 52441088 | bytes 7341952 | tf_op jit(solution)/shard_map/bkc,bikj->bicj/dot_general | solution.py:41
  28.4 11.9 %reshape.179 = bf16[2048,1024]{1,0:T(8,128)(2,1)} reshape(bf16[32,64,16,64]{3,2,1,0:T(8,128)(2,1)} %convert_bitcast_fusion) | data formatting | bytes 8388608 | tf_op jit(solution)/shard_map/reshape | solution.py:43
  40.2 0.0 copy-done
  40.2 5.9 %convolution_bitcast_fusion = f32[512,1024]{0,1:T(8,128)} fusion(bf16[2048,1024]{1,0:T(8,128)(2,1)} %reshape.179, bf16[512,2048]{1,0:T(8,128)(2,1)S(1)} %copy-done), kind=kOutput, calls=%fused_computation.6 | convolution fusion | flops 2147483648 | bytes 8388608 | tf_op jit(solution)/shard_map/dot_general | solution.py:47
  46.1 0.0 all-gather.6.cloned.1.call-update
  46.2 0.2 reduce-scatter.2.cloned.1.call-start
  46.4 0.0 all-gather.4.cloned.1.call-done
  46.4 6.8 %convolution_multiply_fusion = f32[2048,1024]{1,0:T(8,128)} fusion(bf16[512,2048]{1,0:T(8,128)(2,1)S(1)} %copy-done, bf16[512,1024]{1,0:T(8,128)(2,1)} %all-gather.4.cloned.1.call-done), kind=kOutput, calls=%fused_computation.3 | convolution fusion | flops 2149580800 | bytes 11534336 | tf_op jit(solution)/shard_map/dot_general | solution.py:52
  53.2 0.0 reduce-scatter.2.cloned.1.call-update
  53.3 0.7 gather_fusion.1
  54.0 0.6 gather_fusion
  54.6 0.1 iota_compare_fusion.2
  54.7 0.1 broadcast_select_fusion
  54.8 0.0 copy-done.2
  54.8 5.9 %fusion = bf16[512,2048]{0,1:T(8,128)(2,1)} fusion(bf16[2048,1024]{1,0:T(8,128)(2,1)} %reshape.179, bf16[512,1024]{1,0:T(8,128)(2,1)S(1)} %copy-done.2), kind=kOutput, calls=%fused_computation.5 | convolution fusion | flops 2148532224 | bytes 7340032 | tf_op jit(solution)/shard_map/dot_general | solution.py:59
  60.7 4.1 %copy.21 = bf16[512,2048]{1,0:T(8,128)(2,1)} copy(bf16[512,2048]{0,1:T(8,128)(2,1)} %fusion) | data formatting | bytes 4194304
  64.8 70.1 %all-gather.6.cloned.1.call-done = f32[2048,1024]{0,1:T(8,128)} async-done(((f32[512,1024]{0,1:T(8,128)}), f32[2048,1024]{0,1:T(8,128)}) %all-gather.6.cloned.1.call-update) | async-done | bytes 8388624 | tf_op jit(solution)/shard_map/all_gather | solution.py:48
  134.9 10.8 %reshape.198 = f32[4,512,1024]{1,0,2:T(4,128)} reshape(f32[2048,1024]{0,1:T(8,128)} %all-gather.6.cloned.1.call-done) | data formatting | bytes 16777216 | tf_op jit(solution)/shard_map/all_gather | solution.py:48
  145.7 8.5 %reduce_sum.9 = bf16[512,1024]{0,1:T(8,128)(2,1)S(1)} reduce(f32[4,512,1024]{1,0,2:T(4,128)} %reshape.198, f32[]{:T(128)} %constant.48.clone.1), dimensions={0}, to_apply=%region_0.0 | reduce | flops 1572864 | bytes 9437188 | tf_op jit(solution)/shard_map/reduce_sum | solution.py:48
  154.3 0.9 copy.20
  155.1 137.5 %reduce-scatter.2.cloned.1.call-done = f32[32,1024]{1,0:T(8,128)} async-done(((f32[2048,1024]{1,0:T(8,128)}), f32[32,1024]{1,0:T(8,128)}) %reduce-scatter.2.cloned.1.call-update) | async-done | bytes 131088 | tf_op jit(solution)/shard_map/reduce_scatter | solution.py:55
  292.6 1.0 reshape.180
  293.6 0.4 fusion.5
  294.0 0.7 reshape.181
  (7 shorter events, 0.1 us)
Async XLA Ops:
  7.2 33.1 %copy-start = (bf16[512,2048]{1,0:T(8,128)(2,1)S(1)}, bf16[512,2048]{1,0:T(8,128)(2,1)}, u32[]{:S(2)}) copy-start(bf16[512,2048]{1,0:T(8,128)(2,1)} %param.5) | copy-start | bytes 6291460
  7.2 39.2 %all-gather.4.cloned.1.call-start = ((), (), s32[]{:S(2)}) async-start(), calls=%async_computation.1 | async-start | bytes 1310720 | tf_op jit(solution)/shard_map/all_gather | solution.py:49
  7.9 127.0 %all-gather.6.cloned.1.call-start = ((), (), s32[]{:S(2)}) async-start(), calls=%async_computation.3 | async-start | bytes 10485760 | tf_op jit(solution)/shard_map/all_gather | solution.py:48
  8.7 10.6 %copy-start.1 = (s32[32]{0:T(128)S(1)}, s32[32]{0:T(128)}, u32[]{:S(2)}) copy-start(s32[32]{0:T(128)} %param.8) | copy-start | bytes 388
  46.2 246.4 %reduce-scatter.2.cloned.1.call-start = ((), (), s32[]{:S(2)}) async-start(), calls=%async_computation.2 | async-start | bytes 8519680 | tf_op jit(solution)/shard_map/reduce_scatter | solution.py:55
  53.2 1.5 copy-start.2
Sparse Core Ops, SparseCore 0:
  9.8 28.4 all-gather.3
  46.3 88.5 all-gather.5
  139.1 153.4 reduce-scatter.1
